TPU v7x, 512 devices: a whole 4x4x16 slice. The times are simulated.
512 devices in a mesh: seq: 64 (over x, z), head: 8 (over y, core).
Axes of the slice: x: 4, y: 4, z: 16, core: 2. Of those that a mesh axis runs over, the one named last changes fastest.
Arguments:
- tokens: bfloat16 [16384, 4096], P('seq', 'head'), may hold values from -40 to 40
- queries: bfloat16 [16384, 4096], P('seq', 'head'), may hold values from -6 to 6
- key_rows: bfloat16 [16384, 4096], P('seq', 'head'), may hold values from -6 to 6
- values: bfloat16 [16384, 4096], P('seq', 'head'), may hold values from -6 to 6
- log_decay: float32 [32, 16384], P('head', 'seq'), may hold values from -1 to 0
- head_gain: float32 [4096], P('head'), may hold values from 0.5 to 1.5
- expert_gain: float32 [4096], P('head'), may hold values from 0.5 to 1.5
- route_ids: int32 [16384, 2], P('seq'), may hold values from 0 to 31, all different within a row; in each aligned block of 256 rows (0 to 255, 256 to 511, ...) at most 20 rows name the same one
- route_weight: float32 [16384, 2], P('seq'), may hold values from 0.2 to 1
- expert_in: bfloat16 [64, 4096, 1408], P('seq', 'head'), may hold values from -0.09375 to 0.09375
- expert_out: bfloat16 [64, 704, 4096], P('seq', None, 'head'), may hold values from -0.15625 to 0.15625
Outputs:
- mixed: bfloat16 [16384, 4096], P('seq', 'head')
Inputs may be any that keep to these rules, and one draw needn't show every extreme that they name: `route_ids`: within the rows of one device (aligned blocks of 256 tokens) no expert is named by more than 20 tokens, a bound that some block reaches; a token's two experts differ.
All inputs are finite; a program needn't handle non-finite values.
Results may differ from a plain program's by a relative error of at most 0.015.
Values may be sent and summed in bfloat16 or wider, within the bound.
No kernel may reach another device: no remote copies, remote signals or barrier semaphores. Data moves between devices by JAX's collectives and lax.ppermute only.
A program may use at most 64 MiB of HBM per device.

v0:
```python
import jax
import jax.numpy as jnp
from jax import lax
from jax.sharding import PartitionSpec as P

D = 4096
EXPERTS = 32
CAP = 20
CHUNKS = ((0, 10), (10, 20))
EPSILON = 1e-06


def exclusive_scan(decay, state, axis):
    place = lax.axis_index(axis)
    count = lax.axis_size(axis)
    heads, rows, cols = state.shape
    own = jnp.concatenate([state, jnp.broadcast_to(decay[:, None, None], (heads, 1, cols))], axis=1)
    window = own
    before_decay = jnp.ones_like(decay)
    before_state = jnp.zeros_like(state)
    shift = 1
    while shift < count:
        pairs = [(j, j + shift) for j in range(count - shift)]
        got = lax.ppermute(window, axis, pairs)
        valid = place >= shift
        got_state = got[:, :rows, :]
        got_decay = jnp.where(valid, got[:, rows, 0], 1.0)
        before_state = before_decay[:, None, None] * got_state + before_state
        before_decay = before_decay * got_decay
        window_decay = window[:, rows, 0]
        window_state = window_decay[:, None, None] * got_state + window[:, :rows, :]
        window_decay = window_decay * got_decay
        window = jnp.concatenate(
            [window_state, jnp.broadcast_to(window_decay[:, None, None], (heads, 1, cols))], axis=1
        )
        shift *= 2
    return before_state


def per_device(
    tokens,
    queries,
    key_rows,
    values,
    log_decay,
    head_gain,
    expert_gain,
    route_ids,
    route_weight,
    expert_in,
    expert_out,
):
    length = tokens.shape[0]
    local_width = tokens.shape[1]
    heads_here = log_decay.shape[0]
    head_size = queries.shape[1] // heads_here
    score_scale = head_size ** (-0.5)
    query_heads = queries.reshape(length, heads_here, head_size)
    key_heads = key_rows.reshape(length, heads_here, head_size)
    value_heads = values.reshape(length, heads_here, head_size)
    cumulative = jnp.cumsum(log_decay, axis=1)
    causal = (jnp.arange(length)[:, None] >= jnp.arange(length)[None, :])[None]
    scores = (
        jnp.einsum("thd,shd->hts", query_heads, key_heads, preferred_element_type=jnp.float32)
        * score_scale
    )
    spread = cumulative[:, :, None] - cumulative[:, None, :]
    mixing = jnp.where(causal, scores * jnp.exp(jnp.where(causal, spread, 0.0)), 0.0).astype(
        jnp.bfloat16
    )
    inside = jnp.einsum("hts,shd->thd", mixing, value_heads, preferred_element_type=jnp.float32)
    to_end = jnp.exp(cumulative[:, -1:] - cumulative)
    carried_keys = (key_heads.astype(jnp.float32) * to_end.T[:, :, None]).astype(jnp.bfloat16)
    block_state = jnp.einsum(
        "shd,she->hde", carried_keys, value_heads, preferred_element_type=jnp.float32
    )
    block_decay = jnp.exp(cumulative[:, -1])
    entering = exclusive_scan(block_decay, block_state, "seq")
    from_before = jnp.einsum(
        "thd,hde->the",
        query_heads.astype(jnp.float32),
        entering,
        precision=lax.Precision.HIGHEST,
        preferred_element_type=jnp.float32,
    )
    attended = inside + from_before * (jnp.exp(cumulative).T[:, :, None] * score_scale)
    head_rms = lax.rsqrt(jnp.mean(attended * attended, axis=2, keepdims=True) + EPSILON)
    normed_heads = (attended * head_rms).reshape(length, local_width)
    hidden_state = (tokens.astype(jnp.float32) + normed_heads * head_gain).astype(jnp.bfloat16)
    hidden_wide = hidden_state.astype(jnp.float32)
    local_squares = jnp.sum(hidden_wide * hidden_wide, axis=1)
    total_squares = lax.psum(local_squares, "head")
    inverse_rms = lax.rsqrt(total_squares / D + EPSILON)
    expert_input = (hidden_wide * inverse_rms[:, None] * expert_gain).astype(jnp.bfloat16)
    capacity = CAP
    expert_count = EXPERTS
    flat_ids = route_ids.reshape(-1)
    pair_count = flat_ids.shape[0]
    chosen = (flat_ids[:, None] == jnp.arange(expert_count)[None, :]).astype(jnp.float32)
    strictly_before = (jnp.arange(pair_count)[:, None] > jnp.arange(pair_count)[None, :]).astype(
        jnp.float32
    )
    earlier_counts = jnp.dot(
        strictly_before, chosen, precision=lax.Precision.HIGHEST, preferred_element_type=jnp.float32
    )
    slot_index = jnp.sum(earlier_counts * chosen, axis=1).astype(jnp.int32)
    position = (flat_ids * capacity + slot_index).reshape(length, route_ids.shape[1])
    slot_ids = jnp.arange(expert_count * capacity, dtype=jnp.int32)
    picks = position[None, :, :] == slot_ids[:, None, None]
    dispatch_matrix = jnp.any(picks, axis=2).astype(jnp.bfloat16)
    send_rows = jnp.dot(dispatch_matrix, expert_input, preferred_element_type=jnp.float32).astype(
        jnp.bfloat16
    )
    hidden_split = expert_in.shape[0] * lax.axis_size("seq") // expert_count
    send_buffer = jnp.repeat(
        send_rows.reshape(expert_count, 1, capacity, local_width), hidden_split, axis=0
    )
    block_units = expert_out.shape[1]
    pieces = []
    earlier = None
    for lo, hi in CHUNKS:
        arrived = lax.all_to_all(
            send_buffer[:, :, lo:hi], "seq", split_axis=0, concat_axis=1, tiled=True
        )
        blocks_here, sources, item_count, feature_count = arrived.shape
        flat_rows = arrived.reshape(blocks_here, sources * item_count, feature_count)
        partial_sums = jnp.einsum(
            "erd,edh->erh", flat_rows, expert_in, preferred_element_type=jnp.float32
        )
        partial_sums = partial_sums.reshape(blocks_here, sources, item_count, 2, block_units)
        if earlier is not None:
            partial_sums, earlier = lax.optimization_barrier((partial_sums, earlier))
        gate_up = lax.psum(partial_sums.astype(jnp.bfloat16), "head").astype(jnp.float32)
        earlier = gate_up
        activated = (jax.nn.silu(gate_up[:, :, :, 0]) * gate_up[:, :, :, 1]).astype(jnp.bfloat16)
        activated = activated.reshape(blocks_here, sources * item_count, block_units)
        produced = jnp.einsum(
            "erh,ehd->erd", activated, expert_out, preferred_element_type=jnp.float32
        ).astype(jnp.bfloat16)
        computed = produced.reshape(blocks_here, sources, item_count, feature_count)
        returned = lax.all_to_all(computed, "seq", split_axis=1, concat_axis=0, tiled=True)
        pieces.append(
            jnp.sum(
                returned.reshape(expert_count, hidden_split, item_count, local_width).astype(
                    jnp.float32
                ),
                axis=1,
            )
        )
    merged = jnp.concatenate(pieces, axis=1)
    merged = merged.reshape(expert_count * capacity, local_width)
    slot_rows = merged[position]
    expert_mix = jnp.sum(slot_rows * route_weight[:, :, None], axis=1)
    return (hidden_wide + expert_mix).astype(jnp.bfloat16)


def solution(mesh):
    return jax.shard_map(
        per_device,
        mesh=mesh,
        in_specs=(
            P("seq", "head"),
            P("seq", "head"),
            P("seq", "head"),
            P("seq", "head"),
            P("head", "seq"),
            P("head"),
            P("head"),
            P("seq", None),
            P("seq", None),
            P("seq", "head", None),
            P("seq", None, "head"),
        ),
        out_specs=P("seq", "head"),
        check_vma=False,
    )
```

profile of v0, /device:TPU:31, one launch (start us, length us, event | category | flops | bytes accessed | tf_op | source)
XLA Modules:
  0.0 501.7 jit_solution(16637249077426523019)
XLA Ops:
  6.5 0.8 reshape.296
  7.3 1.2 reduce-window.6
  9.2 1.1 copy.119
  10.3 1.2 fusion.29
  11.5 3.5 collective-permute-start
  15.1 14.2 %collective-permute-done = f32[4,129,128]{2,1,0:T(8,128)S(1)} collective-permute-done((f32[4,129,128]{2,1,0:T(8,128)S(1)}, f32[4,129,128]{2,1,0:T(8,128)S(1)}, u32[]{:S(2)}, u32[]{:S(2)}) %collective-permute-start) | collective-permute-done | bytes 264224 | tf_op jit(solution)/shard_map/ppermute | solution.py:24
  29.6 1.9 collective-permute-start.1
  31.7 15.9 %collective-permute-done.1 = f32[4,129,128]{2,1,0:T(8,128)S(1)} collective-permute-done((f32[4,129,128]{2,1,0:T(8,128)S(1)}, f32[4,129,128]{2,1,0:T(8,128)S(1)}, u32[]{:S(2)}, u32[]{:S(2)}) %collective-permute-start.1) | collective-permute-done | bytes 264224 | tf_op jit(solution)/shard_map/ppermute | solution.py:24
  47.9 1.9 collective-permute-start.2
  49.8 27.7 %collective-permute-done.2 = f32[4,129,128]{2,1,0:T(8,128)S(1)} collective-permute-done((f32[4,129,128]{2,1,0:T(8,128)S(1)}, f32[4,129,128]{2,1,0:T(8,128)S(1)}, u32[]{:S(2)}, u32[]{:S(2)}) %collective-permute-start.2) | collective-permute-done | bytes 264224 | tf_op jit(solution)/shard_map/ppermute | solution.py:24
  77.8 1.9 collective-permute-start.3
  79.7 0.1 copy.104
  79.9 0.1 eq.28
  80.0 0.3 fusion.10
  80.3 0.1 convert_element_type.110
  80.5 24.4 %collective-permute-done.3 = f32[4,129,128]{2,1,0:T(8,128)S(1)} collective-permute-done((f32[4,129,128]{2,1,0:T(8,128)S(1)}, f32[4,129,128]{2,1,0:T(8,128)S(1)}, u32[]{:S(2)}, u32[]{:S(2)}) %collective-permute-start.3) | collective-permute-done | bytes 264224 | tf_op jit(solution)/shard_map/ppermute | solution.py:24
  105.3 1.3 collective-permute-start.4
  106.6 0.9 fusion.4
  107.5 7.3 %collective-permute-done.4 = f32[4,129,128]{2,1,0:T(8,128)S(1)} collective-permute-done((f32[4,129,128]{2,1,0:T(8,128)S(1)}, f32[4,129,128]{2,1,0:T(8,128)S(1)}, u32[]{:S(2)}, u32[]{:S(2)}) %collective-permute-start.4) | collective-permute-done | bytes 264224 | tf_op jit(solution)/shard_map/ppermute | solution.py:24
  115.1 0.7 pad_maximum_fusion.6
  115.8 1.3 collective-permute-start.5
  117.2 1.6 fusion.7
  118.8 7.5 %collective-permute-done.5 = f32[4,129,128]{2,1,0:T(8,128)} collective-permute-done((f32[4,129,128]{2,1,0:T(8,128)}, f32[4,129,128]{2,1,0:T(8,128)}, u32[]{:S(2)}, u32[]{:S(2)}) %collective-permute-start.5) | collective-permute-done | bytes 264224 | tf_op jit(solution)/shard_map/ppermute | solution.py:24
  126.3 1.5 multiply_reduce_fusion.1
  127.9 0.2 copy.103
  128.1 0.6 copy-done.5
  128.8 0.2 fusion.20
  128.9 11.9 %psum.21 = f32[256]{0:T(256)S(1)} all-reduce(f32[256]{0:T(256)S(1)} %get-tuple-element.18), channel_id=1, replica_groups=mesh['seq'=64,'head'=8] {'head'}, use_global_device_ids=true, to_apply=%region_6.7 | all-reduce | flops 256 | bytes 2048 | tf_op jit(solution)/shard_map/psum | solution.py:92
  140.8 0.4 convolution_convert_fusion.2
  141.3 0.1 reshape.300
  141.6 1.5 fusion.73
  143.1 62.9 %all_to_all.16 = bf16[64,1,10,512]{3,2,1,0:T(8,128)(2,1)S(1)} all-to-all(bf16[64,1,10,512]{3,2,1,0:T(8,128)(2,1)S(1)} %get-tuple-element.22), channel_id=1, replica_groups=mesh['seq'=64,'head'=8] {'seq'}, dimensions={0} | all-to-all | bytes 1310720 | tf_op jit(solution)/shard_map/all_to_all | solution.py:122
  206.0 10.2 %all-to-all-start.2 = ((bf16[64,1,10,512]{3,2,1,0:T(8,128)(2,1)}), bf16[64,1,10,512]{3,2,1,0:T(8,128)(2,1)}, u32[]{:S(2)}, u32[]{:S(2)}) async-start(bf16[64,1,10,512]{3,2,1,0:T(8,128)(2,1)} %get-tuple-element.23), calls=%async_computation.2 | async-start | bytes 2097152 | tf_op jit(solution)/shard_map/all_to_all | solution.py:122
  216.3 1.6 copy.107
  217.9 4.0 convert_bitcast_fusion
  221.9 81.9 %all-reduce.3.cloned.1.call-done = bf16[1,64,10,2,704]{4,1,3,2,0:T(8,128)(2,1)} async-done(((bf16[1,64,10,2,704]{4,1,3,2,0:T(8,128)(2,1)}), bf16[1,64,10,2,704]{4,1,3,2,0:T(8,128)(2,1)}) %all-reduce.3.cloned.1.call-update) | async-done | bytes 1802256 | tf_op jit(solution)/shard_map/psum | solution.py:133
  303.8 2.0 convert_element_type.115
  305.8 0.6 fusion.1
  306.4 0.6 copy.108
  306.9 0.6 convert_element_type.117
  307.6 0.7 convolution_convert_fusion.1
  308.3 1.2 reshape.303
  309.5 15.4 %all-to-all-start.1 = ((bf16[1,64,10,512]{3,2,0,1:T(8,128)(2,1)}), bf16[1,64,10,512]{3,2,0,1:T(8,128)(2,1)S(1)}, u32[]{:S(2)}, u32[]{:S(2)}) async-start(bf16[1,64,10,512]{3,2,0,1:T(8,128)(2,1)} %bitcast.18), calls=%async_computation.1 | async-start | bytes 2097152 | tf_op jit(solution)/shard_map/all_to_all | solution.py:141
  324.9 3.8 convolution_bitcast_fusion
  328.8 80.3 %all-reduce.5.cloned.1.call-done = bf16[1,64,10,2,704]{4,1,3,2,0:T(8,128)(2,1)} async-done(((bf16[1,64,10,2,704]{4,1,3,2,0:T(8,128)(2,1)}), bf16[1,64,10,2,704]{4,1,3,2,0:T(8,128)(2,1)}) %all-reduce.5.cloned.1.call-update) | async-done | bytes 1802256 | tf_op jit(solution)/shard_map/psum | solution.py:133
  409.0 2.0 convert_element_type.122
  411.0 0.6 fusion
  411.6 0.6 copy.111
  412.2 1.4 convert_element_type.124
  413.6 1.9 convolution_convert_fusion
  415.5 1.2 reshape.305
  416.7 15.5 %all-to-all-start.3 = ((bf16[1,64,10,512]{3,2,0,1:T(8,128)(2,1)}), bf16[1,64,10,512]{3,2,0,1:T(8,128)(2,1)}, u32[]{:S(2)}, u32[]{:S(2)}) async-start(bf16[1,64,10,512]{3,2,0,1:T(8,128)(2,1)} %bitcast.27), calls=%async_computation.3 | async-start | bytes 2097152 | tf_op jit(solution)/shard_map/all_to_all | solution.py:141
  432.3 0.1 copy.114
  432.4 0.1 copy.113
  432.5 0.1 reshape.311
  432.7 0.3 convert_reduce_fusion.1
  433.0 53.0 %all-to-all-done.3 = bf16[1,64,10,512]{3,2,0,1:T(8,128)(2,1)} async-done(((bf16[1,64,10,512]{3,2,0,1:T(8,128)(2,1)}), bf16[1,64,10,512]{3,2,0,1:T(8,128)(2,1)}, u32[]{:S(2)}, u32[]{:S(2)}) %all-to-all-start.3) | async-done | bytes 655392 | tf_op jit(solution)/shard_map/all_to_all | solution.py:141
  485.9 1.6 convert_reduce_fusion
  487.6 1.4 pad_maximum_fusion
  489.0 1.5 reshape.306
  490.4 1.6 gather_fusion
  492.1 0.6 reshape.310
  492.7 1.3 multiply_reduce_fusion
  494.0 0.8 fusion.23
  (76 shorter events, 2.8 us)
Async XLA Ops:
  6.5 301.0 %copy-start = (bf16[1,704,512]{2,1,0:T(8,128)(2,1)S(1)}, bf16[1,704,512]{2,1,0:T(8,128)(2,1)}, u32[]{:S(2)}) copy-start(bf16[1,704,512]{2,1,0:T(8,128)(2,1)} %param.21) | copy-start | bytes 2162692
  11.5 17.8 %collective-permute-start = (f32[4,129,128]{2,1,0:T(8,128)S(1)}, f32[4,129,128]{2,1,0:T(8,128)S(1)}, u32[]{:S(2)}, u32[]{:S(2)}) collective-permute-start(f32[4,129,128]{2,1,0:T(8,128)S(1)} %pad_maximum_fusion.1), channel_id=1, source_target_pairs={{0,8},{8,16},{16,24},{24,32},{32,40},{40,48},{48,56},{56,64},{64,7... | collective-permute-start | bytes 792584 | tf_op jit(solution)/shard_map/ppermute | solution.py:24
  29.4 50.3 %copy-start.8 = (s32[256,2]{0,1:T(2,128)S(1)}, s32[256,2]{0,1:T(2,128)}, u32[]{:S(2)}) copy-start(s32[256,2]{0,1:T(2,128)} %param.18) | copy-start | bytes 6148
  29.6 17.9 %collective-permute-start.1 = (f32[4,129,128]{2,1,0:T(8,128)S(1)}, f32[4,129,128]{2,1,0:T(8,128)S(1)}, u32[]{:S(2)}, u32[]{:S(2)}) collective-permute-start(f32[4,129,128]{2,1,0:T(8,128)S(1)} %pad_maximum_fusion.2), channel_id=1, source_target_pairs={{0,16},{8,24},{16,32},{24,40},{32,48},{40,56},{48,64},{56,72},{64,... | collective-permute-start | bytes 792584 | tf_op jit(solution)/shard_map/ppermute | solution.py:24
  47.9 29.6 %collective-permute-start.2 = (f32[4,129,128]{2,1,0:T(8,128)S(1)}, f32[4,129,128]{2,1,0:T(8,128)S(1)}, u32[]{:S(2)}, u32[]{:S(2)}) collective-permute-start(f32[4,129,128]{2,1,0:T(8,128)S(1)} %pad_maximum_fusion.3), channel_id=1, source_target_pairs={{0,32},{8,40},{16,48},{24,56},{32,64},{40,72},{48,80},{56,88},{64,... | collective-permute-start | bytes 792584 | tf_op jit(solution)/shard_map/ppermute | solution.py:24
  77.8 27.2 %collective-permute-start.3 = (f32[4,129,128]{2,1,0:T(8,128)S(1)}, f32[4,129,128]{2,1,0:T(8,128)S(1)}, u32[]{:S(2)}, u32[]{:S(2)}) collective-permute-start(f32[4,129,128]{2,1,0:T(8,128)S(1)} %pad_maximum_fusion.4), channel_id=1, source_target_pairs={{0,64},{8,72},{16,80},{24,88},{32,96},{40,104},{48,112},{56,120},{... | collective-permute-start | bytes 792584 | tf_op jit(solution)/shard_map/ppermute | solution.py:24
  105.3 9.5 %collective-permute-start.4 = (f32[4,129,128]{2,1,0:T(8,128)S(1)}, f32[4,129,128]{2,1,0:T(8,128)S(1)}, u32[]{:S(2)}, u32[]{:S(2)}) collective-permute-start(f32[4,129,128]{2,1,0:T(8,128)S(1)} %pad_maximum_fusion.5), channel_id=1, source_target_pairs={{0,128},{8,136},{16,144},{24,152},{32,160},{40,168},{48,176},{56,1... | collective-permute-start | bytes 792584 | tf_op jit(solution)/shard_map/ppermute | solution.py:24
  115.0 11.2 %copy-start.6 = (bf16[256,512]{1,0:T(8,128)(2,1)S(1)}, bf16[256,512]{1,0:T(8,128)(2,1)}, u32[]{:S(2)}) copy-start(bf16[256,512]{1,0:T(8,128)(2,1)} %param.12) | copy-start | bytes 786436
  115.8 10.4 %collective-permute-start.5 = (f32[4,129,128]{2,1,0:T(8,128)}, f32[4,129,128]{2,1,0:T(8,128)}, u32[]{:S(2)}, u32[]{:S(2)}) collective-permute-start(f32[4,129,128]{2,1,0:T(8,128)} %pad_maximum_fusion.6), channel_id=1, source_target_pairs={{0,256},{8,264},{16,272},{24,280},{32,288},{40,296},{48,304},{56,3... | collective-permute-start | bytes 792584 | tf_op jit(solution)/shard_map/ppermute | solution.py:24
  126.3 1.8 copy-start.9
  127.8 1.0 copy-start.5
  127.8 13.0 %copy-start.7 = (pred[640,256]{1,0:T(8,128)(4,1)S(1)}, pred[640,256]{1,0:T(8,128)(4,1)}, u32[]{:S(2)}) copy-start(pred[640,256]{1,0:T(8,128)(4,1)} %fusion.4) | copy-start | bytes 491524
  127.8 13.0 %copy-start.11 = (f32[512]{0:T(512)S(1)}, f32[512]{0:T(512)}, u32[]{:S(2)}) copy-start(f32[512]{0:T(512)} %param.17) | copy-start | bytes 6148
  128.9 11.9 %copy-start.3 = (bf16[256,512]{1,0:T(8,128)(2,1)}, bf16[256,512]{1,0:T(8,128)(2,1)S(1)}, u32[]{:S(2)}) copy-start(bf16[256,512]{1,0:T(8,128)(2,1)S(1)} %get-tuple-element.19) | copy-start | bytes 786436
  143.1 73.2 %copy-start.1 = (bf16[1,512,1408]{2,1,0:T(8,128)(2,1)S(1)}, bf16[1,512,1408]{2,1,0:T(8,128)(2,1)}, u32[]{:S(2)}) copy-start(bf16[1,512,1408]{2,1,0:T(8,128)(2,1)} %param.20) | copy-start | bytes 4325380
  206.0 103.5 %all-to-all-start.2 = ((bf16[64,1,10,512]{3,2,1,0:T(8,128)(2,1)}), bf16[64,1,10,512]{3,2,1,0:T(8,128)(2,1)}, u32[]{:S(2)}, u32[]{:S(2)}) async-start(bf16[64,1,10,512]{3,2,1,0:T(8,128)(2,1)} %get-tuple-element.23), calls=%async_computation.2 | async-start | bytes 2097152 | tf_op jit(solution)/shard_map/all_to_all | solution.py:122
  216.2 87.5 %all-reduce.3.cloned.1.call-start = ((), (), s32[]{:S(2)}) async-start(), calls=%async_computation.4 | async-start | bytes 3932160 | tf_op jit(solution)/shard_map/psum | solution.py:133
  308.3 16.7 %copy-start.2 = (bf16[1,512,1408]{1,2,0:T(8,128)(2,1)S(1)}, bf16[1,512,1408]{1,2,0:T(8,128)(2,1)}, u32[]{:S(2)}) copy-start(bf16[1,512,1408]{1,2,0:T(8,128)(2,1)} %copy.107) | copy-start | bytes 4325380
  309.5 107.2 %all-to-all-start.1 = ((bf16[1,64,10,512]{3,2,0,1:T(8,128)(2,1)}), bf16[1,64,10,512]{3,2,0,1:T(8,128)(2,1)S(1)}, u32[]{:S(2)}, u32[]{:S(2)}) async-start(bf16[1,64,10,512]{3,2,0,1:T(8,128)(2,1)} %bitcast.18), calls=%async_computation.1 | async-start | bytes 2097152 | tf_op jit(solution)/shard_map/all_to_all | solution.py:141
  324.9 84.2 %all-reduce.5.cloned.1.call-start = ((), (), s32[]{:S(2)}) async-start(), calls=%async_computation.5 | async-start | bytes 3932160 | tf_op jit(solution)/shard_map/psum | solution.py:133
  415.5 16.8 %copy-start.10 = (f32[256,2]{0,1:T(2,128)S(1)}, f32[256,2]{0,1:T(2,128)}, u32[]{:S(2)}) copy-start(f32[256,2]{0,1:T(2,128)} %param.19) | copy-start | bytes 6148
  416.7 69.2 %all-to-all-start.3 = ((bf16[1,64,10,512]{3,2,0,1:T(8,128)(2,1)}), bf16[1,64,10,512]{3,2,0,1:T(8,128)(2,1)}, u32[]{:S(2)}, u32[]{:S(2)}) async-start(bf16[1,64,10,512]{3,2,0,1:T(8,128)(2,1)} %bitcast.27), calls=%async_computation.3 | async-start | bytes 2097152 | tf_op jit(solution)/shard_map/all_to_all | solution.py:141
  492.0 2.0 copy-start.4
Sparse Core Ops, SparseCore 0:
  222.0 81.7 all-reduce.2
  328.9 80.1 all-reduce.4
where the time goes:
time: 503 us; the launch traced here: 502 us
  waiting for transfers between devices  312 us (62%)
  blocking collectives  74.8 us (15%)
  starting transfers between devices  53.1 us (11%)
  local copies, waits for them, and re-layouts  17.3 us (3%)
  matrix products  15.4 us (3%)
  other arithmetic  15 us (3%)
  between operations  14 us (3%)
    psum x2, waiting for transfers between devices, per_device(): lax.psum(partial_sums.astype(jnp.bfloat16), 'head').astype(jnp.float32)  162 us
    ppermute x6, waiting for transfers between devices, exclusive_scan(): got = lax.ppermute(window, axis, pairs)  97 us
    all_to_all x1, blocking collectives, per_device(): lax.all_to_all(send_buffer[:, :, lo:hi], 'seq', split_axis=0, concat_axis...  62.9 us
    all_to_all x2, waiting for transfers between devices, per_device(): lax.all_to_all(computed, 'seq', split_axis=1, concat_axis=0, tiled=True)  53 us
    all_to_all x2, starting transfers between devices, per_device(): lax.all_to_all(computed, 'seq', split_axis=1, concat_axis=0, tiled=True)  30.9 us
    ppermute x6, starting transfers between devices, exclusive_scan(): got = lax.ppermute(window, axis, pairs)  11.9 us
    psum x1, blocking collectives, per_device(): total_squares = lax.psum(local_squares, 'head')  11.9 us
    all_to_all x1, starting transfers between devices, per_device(): lax.all_to_all(send_buffer[:, :, lo:hi], 'seq', split_axis=0, concat_axis...  10.2 us
  transfers between devices with their start and end apart: 11, of which 9 were waited for; matrix products, arithmetic and copies ran while one was open for 5% of the time, Pallas kernels for 0%

commit v1 on v0

--- a/solution.py
+++ b/solution.py
@@ -119,8 +119,14 @@
     pieces = []
     earlier = None
     for lo, hi in CHUNKS:
-        arrived = lax.all_to_all(
-            send_buffer[:, :, lo:hi], "seq", split_axis=0, concat_axis=1, tiled=True
+        arrived = jnp.concatenate(
+            lax.all_to_all(
+                jnp.stack(jnp.split(send_buffer[:, :, lo:hi], lax.axis_size("seq"), axis=0)),
+                "seq",
+                0,
+                0,
+            ),
+            axis=1,
         )
         blocks_here, sources, item_count, feature_count = arrived.shape
         flat_rows = arrived.reshape(blocks_here, sources * item_count, feature_count)

time: 503 us -> 540 us (1.074)
  local copies, waits for them, and re-layouts: 17.3 us -> 54.4 us
    unnamed x29 -> x91, local copies, waits for them, and re-layouts: 2.64 us -> 40.6 us
where the time goes in v1:
time: 540 us; the launch traced here: 539 us
  waiting for transfers between devices  312 us (58%)
  blocking collectives  74.8 us (14%)
  local copies, waits for them, and re-layouts  54.4 us (10%)
  starting transfers between devices  53.4 us (10%)
  matrix products  15.5 us (3%)
  other arithmetic  14.7 us (3%)
  between operations  14 us (3%)
    psum x2, waiting for transfers between devices, per_device(): lax.psum(partial_sums.astype(jnp.bfloat16), 'head').astype(jnp.float32)  162 us
    ppermute x6, waiting for transfers between devices, exclusive_scan(): got = lax.ppermute(window, axis, pairs)  96.8 us
    all_to_all x1, blocking collectives, per_device(): lax.all_to_all(jnp.stack(jnp.split(send_buffer[:, :, lo:hi], lax.axis_siz...  62.9 us
    all_to_all x2, waiting for transfers between devices, per_device(): lax.all_to_all(computed, 'seq', split_axis=1, concat_axis=0, tiled=True)  53 us
    unnamed x91, local copies, waits for them, and re-layouts  40.6 us
    all_to_all x2, starting transfers between devices, per_device(): lax.all_to_all(computed, 'seq', split_axis=1, concat_axis=0, tiled=True)  31.1 us
    ppermute x6, starting transfers between devices, exclusive_scan(): got = lax.ppermute(window, axis, pairs)  11.9 us
    psum x1, blocking collectives, per_device(): total_squares = lax.psum(local_squares, 'head')  11.9 us
  transfers between devices with their start and end apart: 11, of which 9 were waited for; matrix products, arithmetic and copies ran while one was open for 5% of the time, Pallas kernels for 0%

profile of v1, /device:TPU:31, one launch (start us, length us, event | category | flops | bytes accessed | tf_op | source)
XLA Modules:
  0.0 538.9 jit_solution(4526771121444809620)
XLA Ops:
  6.5 0.8 reshape.286
  7.3 1.2 reduce-window.6
  9.3 1.0 reshape.285
  10.7 1.2 fusion.30
  12.0 3.5 collective-permute-start
  15.6 14.2 %collective-permute-done = f32[4,129,128]{2,1,0:T(8,128)S(1)} collective-permute-done((f32[4,129,128]{2,1,0:T(8,128)S(1)}, f32[4,129,128]{2,1,0:T(8,128)S(1)}, u32[]{:S(2)}, u32[]{:S(2)}) %collective-permute-start) | collective-permute-done | bytes 264224 | tf_op jit(solution)/shard_map/ppermute | solution.py:24
  30.1 1.9 collective-permute-start.1
  32.1 16.0 %collective-permute-done.1 = f32[4,129,128]{2,1,0:T(8,128)S(1)} collective-permute-done((f32[4,129,128]{2,1,0:T(8,128)S(1)}, f32[4,129,128]{2,1,0:T(8,128)S(1)}, u32[]{:S(2)}, u32[]{:S(2)}) %collective-permute-start.1) | collective-permute-done | bytes 264224 | tf_op jit(solution)/shard_map/ppermute | solution.py:24
  48.4 1.9 collective-permute-start.2
  50.3 27.6 %collective-permute-done.2 = f32[4,129,128]{2,1,0:T(8,128)S(1)} collective-permute-done((f32[4,129,128]{2,1,0:T(8,128)S(1)}, f32[4,129,128]{2,1,0:T(8,128)S(1)}, u32[]{:S(2)}, u32[]{:S(2)}) %collective-permute-start.2) | collective-permute-done | bytes 264224 | tf_op jit(solution)/shard_map/ppermute | solution.py:24
  78.2 1.9 collective-permute-start.3
  81.0 24.5 %collective-permute-done.3 = f32[4,129,128]{2,1,0:T(8,128)S(1)} collective-permute-done((f32[4,129,128]{2,1,0:T(8,128)S(1)}, f32[4,129,128]{2,1,0:T(8,128)S(1)}, u32[]{:S(2)}, u32[]{:S(2)}) %collective-permute-start.3) | collective-permute-done | bytes 264224 | tf_op jit(solution)/shard_map/ppermute | solution.py:24
  105.8 1.3 collective-permute-start.4
  107.1 0.9 fusion.4
  108.0 7.4 %collective-permute-done.4 = f32[4,129,128]{2,1,0:T(8,128)S(1)} collective-permute-done((f32[4,129,128]{2,1,0:T(8,128)S(1)}, f32[4,129,128]{2,1,0:T(8,128)S(1)}, u32[]{:S(2)}, u32[]{:S(2)}) %collective-permute-start.4) | collective-permute-done | bytes 264224 | tf_op jit(solution)/shard_map/ppermute | solution.py:24
  115.7 1.3 collective-permute-start.5
  117.0 1.8 fusion.7
  118.8 7.1 %collective-permute-done.5 = f32[4,129,128]{2,1,0:T(8,128)} collective-permute-done((f32[4,129,128]{2,1,0:T(8,128)S(1)}, f32[4,129,128]{2,1,0:T(8,128)}, u32[]{:S(2)}, u32[]{:S(2)}) %collective-permute-start.5) | collective-permute-done | bytes 264224 | tf_op jit(solution)/shard_map/ppermute | solution.py:24
  125.9 1.5 multiply_reduce_fusion.1
  127.8 0.6 copy-done.5
  128.6 11.9 %psum.21 = f32[256]{0:T(256)S(1)} all-reduce(f32[256]{0:T(256)S(1)} %get-tuple-element.18), channel_id=1, replica_groups=mesh['seq'=64,'head'=8] {'head'}, use_global_device_ids=true, to_apply=%region_6.7 | all-reduce | flops 256 | bytes 2048 | tf_op jit(solution)/shard_map/psum | solution.py:92
  141.2 0.6 constant_dynamic-update-slice_fusion.63
  142.4 0.6 constant_dynamic-update-slice_fusion.61
  144.8 0.6 constant_dynamic-update-slice_fusion.57
  147.3 0.6 constant_dynamic-update-slice_fusion.53
  149.1 0.6 constant_dynamic-update-slice_fusion.50
  151.5 0.6 constant_dynamic-update-slice_fusion.46
  153.3 0.6 constant_dynamic-update-slice_fusion.43
  154.5 0.6 constant_dynamic-update-slice_fusion.41
  155.1 0.6 constant_dynamic-update-slice_fusion.40
  156.9 0.6 constant_dynamic-update-slice_fusion.37
  157.5 0.6 constant_dynamic-update-slice_fusion.36
  158.2 0.6 constant_dynamic-update-slice_fusion.35
  158.8 0.6 constant_dynamic-update-slice_fusion.34
  159.4 0.6 constant_dynamic-update-slice_fusion.33
  161.8 0.6 constant_dynamic-update-slice_fusion.29
  169.1 0.6 constant_dynamic-update-slice_fusion.17
  172.7 0.6 constant_dynamic-update-slice_fusion.11
  173.9 0.6 constant_dynamic-update-slice_fusion.9
  179.9 62.9 %all_to_all.28 = bf16[64,1,1,10,512]{4,3,2,1,0:T(8,128)(2,1)S(1)} all-to-all(bf16[64,1,1,10,512]{4,3,2,1,0:T(8,128)(2,1)S(1)} %get-tuple-element.22), channel_id=1, replica_groups=mesh['seq'=64,'head'=8] {'seq'}, dimensions={0} | all-to-all | bytes 1310720 | tf_op jit(solution)/shard_map/all_to_all | solution.py:123
  242.9 10.4 %all-to-all-start.2 = ((bf16[64,1,1,10,512]{4,3,2,1,0:T(8,128)(2,1)}), bf16[64,1,1,10,512]{4,3,2,1,0:T(8,128)(2,1)}, u32[]{:S(2)}, u32[]{:S(2)}) async-start(bf16[64,1,1,10,512]{4,3,2,1,0:T(8,128)(2,1)} %get-tuple-element.23), calls=%async_computation.2 | async-start | bytes 2097152 | tf_op jit(solution)/shard_map/all_to_all | solution.py:123
  253.3 1.6 copy.2662
  254.9 3.9 convert_bitcast_fusion
  258.9 81.9 %all-reduce.3.cloned.1.call-done = bf16[1,64,10,2,704]{4,1,3,2,0:T(8,128)(2,1)} async-done(((bf16[1,64,10,2,704]{4,1,3,2,0:T(8,128)(2,1)}), bf16[1,64,10,2,704]{4,1,3,2,0:T(8,128)(2,1)}) %all-reduce.3.cloned.1.call-update) | async-done | bytes 1802256 | tf_op jit(solution)/shard_map/psum | solution.py:139
  340.8 2.0 convert_element_type.115
  344.0 0.6 convert_element_type.117
  344.6 0.7 convolution_convert_fusion.1
  345.3 1.2 reshape.293
  346.5 15.5 %all-to-all-start.1 = ((bf16[1,64,10,512]{3,2,0,1:T(8,128)(2,1)}), bf16[1,64,10,512]{3,2,0,1:T(8,128)(2,1)S(1)}, u32[]{:S(2)}, u32[]{:S(2)}) async-start(bf16[1,64,10,512]{3,2,0,1:T(8,128)(2,1)} %bitcast.81), calls=%async_computation.1 | async-start | bytes 2097152 | tf_op jit(solution)/shard_map/all_to_all | solution.py:147
  362.1 3.8 convolution_bitcast_fusion
  365.9 80.3 %all-reduce.5.cloned.1.call-done = bf16[1,64,10,2,704]{4,1,3,2,0:T(8,128)(2,1)} async-done(((bf16[1,64,10,2,704]{4,1,3,2,0:T(8,128)(2,1)}), bf16[1,64,10,2,704]{4,1,3,2,0:T(8,128)(2,1)}) %all-reduce.5.cloned.1.call-update) | async-done | bytes 1802256 | tf_op jit(solution)/shard_map/psum | solution.py:139
  446.3 2.0 convert_element_type.122
  449.4 1.4 convert_element_type.124
  450.8 1.9 convolution_convert_fusion
  452.7 1.2 reshape.295
  453.9 15.5 %all-to-all-start.3 = ((bf16[1,64,10,512]{3,2,0,1:T(8,128)(2,1)}), bf16[1,64,10,512]{3,2,0,1:T(8,128)(2,1)}, u32[]{:S(2)}, u32[]{:S(2)}) async-start(bf16[1,64,10,512]{3,2,0,1:T(8,128)(2,1)} %bitcast.153), calls=%async_computation.3 | async-start | bytes 2097152 | tf_op jit(solution)/shard_map/all_to_all | solution.py:147
  470.2 53.0 %all-to-all-done.3 = bf16[1,64,10,512]{3,2,0,1:T(8,128)(2,1)} async-done(((bf16[1,64,10,512]{3,2,0,1:T(8,128)(2,1)}), bf16[1,64,10,512]{3,2,0,1:T(8,128)(2,1)}, u32[]{:S(2)}, u32[]{:S(2)}) %all-to-all-start.3) | async-done | bytes 655392 | tf_op jit(solution)/shard_map/all_to_all | solution.py:147
  523.2 1.6 convert_reduce_fusion
  524.8 1.4 pad_maximum_fusion
  526.2 1.5 reshape.296
  527.7 1.6 gather_fusion
  529.3 0.6 reshape.300
  529.9 1.3 multiply_reduce_fusion
  531.3 0.8 fusion.22
  (138 shorter events, 35.6 us)
Async XLA Ops:
  6.5 338.1 %copy-start = (bf16[1,704,512]{2,1,0:T(8,128)(2,1)S(1)}, bf16[1,704,512]{2,1,0:T(8,128)(2,1)}, u32[]{:S(2)}) copy-start(bf16[1,704,512]{2,1,0:T(8,128)(2,1)} %param.21) | copy-start | bytes 2162692
  12.0 17.8 %collective-permute-start = (f32[4,129,128]{2,1,0:T(8,128)S(1)}, f32[4,129,128]{2,1,0:T(8,128)S(1)}, u32[]{:S(2)}, u32[]{:S(2)}) collective-permute-start(f32[4,129,128]{2,1,0:T(8,128)S(1)} %pad_maximum_fusion.1), channel_id=1, source_target_pairs={{0,8},{8,16},{16,24},{24,32},{32,40},{40,48},{48,56},{56,64},{64,7... | collective-permute-start | bytes 792584 | tf_op jit(solution)/shard_map/ppermute | solution.py:24
  30.1 50.0 %copy-start.8 = (s32[256,2]{0,1:T(2,128)S(1)}, s32[256,2]{0,1:T(2,128)}, u32[]{:S(2)}) copy-start(s32[256,2]{0,1:T(2,128)} %param.18) | copy-start | bytes 6148
  30.1 17.9 %collective-permute-start.1 = (f32[4,129,128]{2,1,0:T(8,128)S(1)}, f32[4,129,128]{2,1,0:T(8,128)S(1)}, u32[]{:S(2)}, u32[]{:S(2)}) collective-permute-start(f32[4,129,128]{2,1,0:T(8,128)S(1)} %pad_maximum_fusion.2), channel_id=1, source_target_pairs={{0,16},{8,24},{16,32},{24,40},{32,48},{40,56},{48,64},{56,72},{64,... | collective-permute-start | bytes 792584 | tf_op jit(solution)/shard_map/ppermute | solution.py:24
  48.4 29.5 %collective-permute-start.2 = (f32[4,129,128]{2,1,0:T(8,128)S(1)}, f32[4,129,128]{2,1,0:T(8,128)S(1)}, u32[]{:S(2)}, u32[]{:S(2)}) collective-permute-start(f32[4,129,128]{2,1,0:T(8,128)S(1)} %pad_maximum_fusion.3), channel_id=1, source_target_pairs={{0,32},{8,40},{16,48},{24,56},{32,64},{40,72},{48,80},{56,88},{64,... | collective-permute-start | bytes 792584 | tf_op jit(solution)/shard_map/ppermute | solution.py:24
  78.2 27.2 %collective-permute-start.3 = (f32[4,129,128]{2,1,0:T(8,128)S(1)}, f32[4,129,128]{2,1,0:T(8,128)S(1)}, u32[]{:S(2)}, u32[]{:S(2)}) collective-permute-start(f32[4,129,128]{2,1,0:T(8,128)S(1)} %pad_maximum_fusion.4), channel_id=1, source_target_pairs={{0,64},{8,72},{16,80},{24,88},{32,96},{40,104},{48,112},{56,120},{... | collective-permute-start | bytes 792584 | tf_op jit(solution)/shard_map/ppermute | solution.py:24
  105.8 9.6 %collective-permute-start.4 = (f32[4,129,128]{2,1,0:T(8,128)S(1)}, f32[4,129,128]{2,1,0:T(8,128)S(1)}, u32[]{:S(2)}, u32[]{:S(2)}) collective-permute-start(f32[4,129,128]{2,1,0:T(8,128)S(1)} %pad_maximum_fusion.5), channel_id=1, source_target_pairs={{0,128},{8,136},{16,144},{24,152},{32,160},{40,168},{48,176},{56,1... | collective-permute-start | bytes 792584 | tf_op jit(solution)/shard_map/ppermute | solution.py:24
  115.7 10.3 %collective-permute-start.5 = (f32[4,129,128]{2,1,0:T(8,128)S(1)}, f32[4,129,128]{2,1,0:T(8,128)}, u32[]{:S(2)}, u32[]{:S(2)}) collective-permute-start(f32[4,129,128]{2,1,0:T(8,128)S(1)} %pad_maximum_fusion.6), channel_id=1, source_target_pairs={{0,256},{8,264},{16,272},{24,280},{32,288},{40,296},{48,304},{56,3... | collective-permute-start | bytes 792584 | tf_op jit(solution)/shard_map/ppermute | solution.py:24
  117.0 8.9 %copy-start.6 = (bf16[256,512]{1,0:T(8,128)(2,1)S(1)}, bf16[256,512]{1,0:T(8,128)(2,1)}, u32[]{:S(2)}) copy-start(bf16[256,512]{1,0:T(8,128)(2,1)} %param.12) | copy-start | bytes 786436
  127.4 1.0 copy-start.5
  127.5 0.9 copy-start.9
  127.5 13.0 %copy-start.7 = (pred[640,256]{1,0:T(8,128)(4,1)S(1)}, pred[640,256]{1,0:T(8,128)(4,1)}, u32[]{:S(2)}) copy-start(pred[640,256]{1,0:T(8,128)(4,1)} %fusion.4) | copy-start | bytes 491524
  127.5 13.0 %copy-start.11 = (f32[512]{0:T(512)S(1)}, f32[512]{0:T(512)}, u32[]{:S(2)}) copy-start(f32[512]{0:T(512)} %param.17) | copy-start | bytes 6148
  128.6 11.9 %copy-start.3 = (bf16[256,512]{1,0:T(8,128)(2,1)}, bf16[256,512]{1,0:T(8,128)(2,1)S(1)}, u32[]{:S(2)}) copy-start(bf16[256,512]{1,0:T(8,128)(2,1)S(1)} %get-tuple-element.19) | copy-start | bytes 786436
  242.9 10.4 %copy-start.1 = (bf16[1,512,1408]{2,1,0:T(8,128)(2,1)S(1)}, bf16[1,512,1408]{2,1,0:T(8,128)(2,1)}, u32[]{:S(2)}) copy-start(bf16[1,512,1408]{2,1,0:T(8,128)(2,1)} %param.20) | copy-start | bytes 4325380
  242.9 103.6 %all-to-all-start.2 = ((bf16[64,1,1,10,512]{4,3,2,1,0:T(8,128)(2,1)}), bf16[64,1,1,10,512]{4,3,2,1,0:T(8,128)(2,1)}, u32[]{:S(2)}, u32[]{:S(2)}) async-start(bf16[64,1,1,10,512]{4,3,2,1,0:T(8,128)(2,1)} %get-tuple-element.23), calls=%async_computation.2 | async-start | bytes 2097152 | tf_op jit(solution)/shard_map/all_to_all | solution.py:123
  253.3 87.5 %all-reduce.3.cloned.1.call-start = ((), (), s32[]{:S(2)}) async-start(), calls=%async_computation.4 | async-start | bytes 3932160 | tf_op jit(solution)/shard_map/psum | solution.py:139
  345.3 16.8 %copy-start.2 = (bf16[1,512,1408]{1,2,0:T(8,128)(2,1)S(1)}, bf16[1,512,1408]{1,2,0:T(8,128)(2,1)}, u32[]{:S(2)}) copy-start(bf16[1,512,1408]{1,2,0:T(8,128)(2,1)} %copy.2662) | copy-start | bytes 4325380
  346.5 107.4 %all-to-all-start.1 = ((bf16[1,64,10,512]{3,2,0,1:T(8,128)(2,1)}), bf16[1,64,10,512]{3,2,0,1:T(8,128)(2,1)S(1)}, u32[]{:S(2)}, u32[]{:S(2)}) async-start(bf16[1,64,10,512]{3,2,0,1:T(8,128)(2,1)} %bitcast.81), calls=%async_computation.1 | async-start | bytes 2097152 | tf_op jit(solution)/shard_map/all_to_all | solution.py:147
  362.0 84.2 %all-reduce.5.cloned.1.call-start = ((), (), s32[]{:S(2)}) async-start(), calls=%async_computation.5 | async-start | bytes 3932160 | tf_op jit(solution)/shard_map/psum | solution.py:139
  452.7 16.8 %copy-start.10 = (f32[256,2]{0,1:T(2,128)S(1)}, f32[256,2]{0,1:T(2,128)}, u32[]{:S(2)}) copy-start(f32[256,2]{0,1:T(2,128)} %param.19) | copy-start | bytes 6148
  453.9 69.2 %all-to-all-start.3 = ((bf16[1,64,10,512]{3,2,0,1:T(8,128)(2,1)}), bf16[1,64,10,512]{3,2,0,1:T(8,128)(2,1)}, u32[]{:S(2)}, u32[]{:S(2)}) async-start(bf16[1,64,10,512]{3,2,0,1:T(8,128)(2,1)} %bitcast.153), calls=%async_computation.3 | async-start | bytes 2097152 | tf_op jit(solution)/shard_map/all_to_all | solution.py:147
  529.3 2.0 copy-start.4
Sparse Core Ops, SparseCore 0:
  259.0 81.7 all-reduce.2
  366.1 80.1 all-reduce.4
